TPU v7x, 256 devices: a whole 4x4x8 slice. The times are simulated.
256 devices in a mesh: gx: 16 (over y, x), gy: 16 (over z, core).
Axes of the slice: x: 4, y: 4, z: 8, core: 2. Of those that a mesh axis runs over, the one named last changes fastest.
Arguments:
- energy: float32 [256, 2048, 128], P('gx', 'gy'), may hold values from 1 to 5
- coupling: float32 [256, 2048, 128], P('gx', 'gy'), may hold values from 4000 to 40000
Outputs:
- energy_next: float32 [256, 2048, 128], P('gx', 'gy')
All inputs are finite; a program needn't handle non-finite values.
Results may differ from a plain program's by a relative error of at most 0.0003.
Values sent between devices are 32-bit elements; how exact they have to be, the bound alone decides.
No kernel may reach another device: no remote copies, remote signals or barrier semaphores. Data moves between devices by JAX's collectives and lax.ppermute only.
A program may use at most 64 MiB of HBM per device.

v0:
```python
import jax
import jax.numpy as jnp
from jax import lax
from jax.sharding import PartitionSpec as P

y_weight = 0.15


def with_halo(shard, sides, width):
    for axis, dim in sides:
        size, length = (lax.axis_size(axis), shard.shape[dim])
        up = [(i, (i + 1) % size) for i in range(size - 1)]
        down = [(j, i) for i, j in up]
        last = lax.slice_in_dim(shard, length - width, length, axis=dim)
        initial = lax.slice_in_dim(shard, 0, width, axis=dim)
        before = lax.ppermute(last, axis, up)
        after = lax.ppermute(initial, axis, down)
        shard = jnp.concatenate([before, shard, after], axis=dim)
    return shard


def shifted(value, axis, steps):
    count = lax.axis_size(axis)
    initial, last = (max(0, -steps), min(count, count - steps))
    return lax.ppermute(value, axis, [(source, source + steps) for source in range(initial, last)])


def many_solve(diag_part, lower_part, upper_part, sources):

    def forward(running, row):
        prev_ratio, prev_value = running
        diag_row, lower_row, upper_row, source_row = row
        denom = diag_row - lower_row * prev_ratio
        new_ratio = upper_row / denom
        new_value = (source_row - lower_row[None] * prev_value) / denom[None]
        return ((new_ratio, new_value), (new_ratio, new_value))

    start = (jnp.zeros(diag_part.shape[1:], jnp.float32), jnp.zeros(sources.shape[1:], jnp.float32))
    _, (ratios, values) = lax.scan(forward, start, (diag_part, lower_part, upper_part, sources))

    def backward(later_value, row):
        ratio_row, value_row = row
        result = value_row - ratio_row[None] * later_value
        return (result, result)

    _, solved = lax.scan(
        backward, jnp.zeros(sources.shape[1:], jnp.float32), (ratios, values), reverse=True
    )
    return solved


def body(energy, coupling):
    padded = with_halo(energy, (("gy", 1),), 1)
    source_term = energy + y_weight * (padded[:, :-2] - 2.0 * energy + padded[:, 2:])
    height = energy.shape[0]
    inner_diag = 1.0 + coupling[: height - 1] + coupling[1:height]
    inner_lower = -coupling[: height - 1]
    inner_upper = -coupling[1:height]
    blank = jnp.zeros_like(coupling[: height - 1])
    left_source = jnp.concatenate([coupling[:1], blank[1:]], 0)
    right_source = jnp.concatenate([blank[1:], coupling[height - 1 : height]], 0)
    sources = jnp.stack([source_term[: height - 1], left_source, right_source], 1)
    solved = many_solve(inner_diag, inner_lower, inner_upper, sources)
    local_part = solved[:, 0]
    left_reply = solved[:, 1]
    right_reply = solved[:, 2]
    first_rows = jnp.stack([local_part[0], left_reply[0], right_reply[0], coupling[0]], 0)
    following = shifted(first_rows, "gx", -1)
    next_local = following[0]
    next_left = following[1]
    next_right = following[2]
    next_face = following[3]
    own_face = coupling[height - 1]
    position = lax.axis_index("gx")
    lower_coef = jnp.where(position == 0, 0.0, -own_face * left_reply[height - 2])
    middle = 1.0 + own_face + next_face - own_face * right_reply[height - 2] - next_face * next_left
    upper_coef = -next_face * next_right
    target = source_term[height - 1] + own_face * local_part[height - 2] + next_face * next_local
    bundle = jnp.stack([lower_coef, middle, upper_coef, target], 0)[None]
    gathered = lax.all_gather(bundle, "gx", axis=0, tiled=True)
    whole = many_solve(gathered[:, 1], gathered[:, 0], gathered[:, 2], gathered[:, 3][:, None])
    last_value = lax.dynamic_index_in_dim(whole[:, 0], position, 0, keepdims=False)
    previous = shifted(last_value, "gx", 1)
    interior = local_part + left_reply * previous[None] + right_reply * last_value[None]
    return jnp.concatenate([interior, last_value[None]], 0)


def solution(mesh):
    in_specs = (P("gx", "gy", None), P("gx", "gy", None))
    out_specs = P("gx", "gy", None)
    return jax.shard_map(body, mesh=mesh, in_specs=in_specs, out_specs=out_specs, check_vma=False)
```

profile of v0, /device:TPU:8, one launch (start us, length us, event | category | flops | bytes accessed | tf_op | source)
XLA Modules:
  0.0 257.6 jit_solution(15537490057633315321)
XLA Ops:
  7.4 1.7 collective-permute-start
  11.4 3.7 %select_bitcast_fusion = (f32[15,1,128,128]{3,2,0,1:T(8,128)}, f32[15,128,128]{2,1,0:T(8,128)}, f32[15,128,128]{2,1,0:T(8,128)}, f32[15,128,128]{2,1,0:T(8,128)}) fusion(f32[16,128,128]{2,1,0:T(8,128)} %param.11, pred[15]{0:T(512)(128)(4,1)} %constant.130.clone.1), kind=kLoop, calls=%fused_computation.44 | loop fusion | flops 1228800 | bytes 5898255 | tf_op jit(solution)/shard_map/stack | solution.py:62
  18.2 1.9 broadcast.28.clone
  21.2 34.4 %while.68 = (s32[]{:T(128)}, f32[128,128]{1,0:T(8,128)S(1)}, f32[3,128,128]{2,1,0:T(8,128)S(1)}, f32[15,128,128]{2,1,0:T(8,128)}, f32[15,3,128,128]{3,2,1,0:T(8,...) while((s32[]{:T(128)}, f32[128,128]{1,0:T(8,128)S(1)}, ...), condition=%wide.region_1.2_spmd.clone, body=%wide.region_0.1_spmd.clone.sunk | while | flops 262147 | bytes 1442936 | solution.py:39
  55.9 28.5 %while.69 = (s32[]{:T(128)}, f32[3,128,128]{2,1,0:T(8,128)S(1)}, f32[15,3,128,128]{3,2,1,0:T(8,128)S(1)}, f32[15,3,128,128]{3,2,1,0:T(8,128)}, f32[15,128,128]{2...) while((s32[]{:T(128)}, f32[3,128,128]{2,1,0:T(8,128)S(1)}, f32[15,3,128,128]{3,2,1,0:T(8,128)S(1)}, ...), condition=%wide.region_3.4_spmd.clone, body=%wide.region_2.3_spmd.clone.sunk | while | flops 147460 | bytes 983155 | solution.py:46
  84.5 4.6 %collective-permute-start.2 = (f32[4,128,128]{2,1,0:T(8,128)S(1)}, f32[4,128,128]{2,1,0:T(8,128)S(1)}, u32[]{:S(2)}, u32[]{:S(2)}) collective-permute-start(f32[4,128,128]{2,1,0:T(8,128)S(1)} %pad_maximum_fusion.4), channel_id=1, source_target_pairs={{16,0},{32,16},{48,32},{64,48},{80,64},{96,80},{112,96},{128,112},... | collective-permute-start | bytes 786440 | tf_op jit(solution)/shard_map/ppermute | solution.py:25
  89.1 4.8 %collective-permute-done.2 = f32[4,128,128]{2,1,0:T(8,128)S(1)} collective-permute-done((f32[4,128,128]{2,1,0:T(8,128)S(1)}, f32[4,128,128]{2,1,0:T(8,128)S(1)}, u32[]{:S(2)}, u32[]{:S(2)}) %collective-permute-start.2) | collective-permute-done | bytes 262176 | tf_op jit(solution)/shard_map/ppermute | solution.py:25
  95.6 63.9 %all-gather.3.cloned.1.call-done = f32[64,128,128]{2,1,0:T(8,128)} async-done(((f32[4,128,128]{2,1,0:T(8,128)}), f32[64,128,128]{2,1,0:T(8,128)}) %all-gather.3.cloned.1.call-update) | async-done | bytes 4194320 | tf_op jit(solution)/shard_map/all_gather | solution.py:80
  159.5 4.3 %fusion.15 = (f32[16,1,128,128]{3,2,1,0:T(8,128)}, f32[16,128,128]{2,1,0:T(8,128)}, f32[16,128,128]{2,1,0:T(8,128)}, f32[16,128,128]{2,1,0:T(8,128)}) fusion(f32[16,4,128,128]{3,2,1,0:T(8,128)} %bitcast.136), kind=kLoop, calls=%fused_computation.66 | loop fusion | bytes 8388608 | tf_op jit(solution)/shard_map/slice | solution.py:81
  164.9 49.7 %while.70 = (s32[]{:T(128)}, f32[128,128]{1,0:T(8,128)S(1)}, f32[1,128,128]{2,1,0:T(8,128)S(1)}, f32[16,128,128]{2,1,0:T(8,128)}, f32[16,1,128,128]{3,2,1,0:T(8,...) while((s32[]{:T(128)}, f32[128,128]{1,0:T(8,128)S(1)}, ...), condition=%wide.region_5.6_spmd.clone, body=%wide.region_4.5_spmd.clone.sunk | while | flops 180227 | bytes 854135 | solution.py:39
  168.0 1.6 bitcast_dynamic-update-slice_fusion.16
  171.1 1.6 bitcast_dynamic-update-slice_fusion.16
  174.2 1.6 bitcast_dynamic-update-slice_fusion.16
  183.5 1.6 bitcast_dynamic-update-slice_fusion.16
  186.6 1.6 bitcast_dynamic-update-slice_fusion.16
  189.7 1.6 bitcast_dynamic-update-slice_fusion.16
  192.9 1.6 bitcast_dynamic-update-slice_fusion.16
  194.4 1.6 bitcast_dynamic-update-slice_fusion.15
  199.1 1.6 bitcast_dynamic-update-slice_fusion.16
  208.4 1.6 bitcast_dynamic-update-slice_fusion.16
  211.5 1.6 bitcast_dynamic-update-slice_fusion.16
  215.7 24.7 %while.71 = (s32[]{:T(128)}, f32[1,128,128]{2,1,0:T(8,128)S(1)}, f32[16,1,128,128]{3,2,1,0:T(8,128)}, f32[16,1,128,128]{3,2,1,0:T(8,128)}, f32[16,128,128]{2,1,0:T(8,128)}, /*index=5*/s32[]{:T(128)}, s32[]{:T(128)}, s32[]{:T(128)}) while((s32[]{:T(128)}, f32[1,128,128]{2,1,0:T(8,128)S(1)}, f32[16,1,128,128]{3,2,1,0:T(8,128)}, ...), condition=%wide.region_7.8_spmd.clone, body=%wide.region_6.7_spmd.clone.sunk | while | flops 49156 | bytes 327791 | solution.py:46
  241.2 2.2 collective-permute-start.3
  243.4 6.1 %collective-permute-done.3 = f32[128,128]{1,0:T(8,128)S(1)} collective-permute-done((f32[128,128]{1,0:T(8,128)S(1)}, f32[128,128]{1,0:T(8,128)S(1)}, u32[]{:S(2)}, u32[]{:S(2)}) %collective-permute-start.3) | collective-permute-done | bytes 65568 | tf_op jit(solution)/shard_map/ppermute | solution.py:25
  (134 shorter events, 133.4 us)
Async XLA Ops:
  6.5 153.0 %all-gather.3.cloned.1.call-start = ((), (), s32[]{:S(2)}) async-start(), calls=%async_computation | async-start | bytes 4456448 | tf_op jit(solution)/shard_map/all_gather | solution.py:80
  7.4 8.7 %collective-permute-start = (f32[16,1,128]{2,1,0:T(1,128)S(1)}, f32[16,1,128]{2,1,0:T(1,128)S(1)}, u32[]{:S(2)}, u32[]{:S(2)}) collective-permute-start(f32[16,1,128]{2,1,0:T(1,128)S(1)} %get-tuple-element.509), channel_id=1, source_target_pairs={{0,1},{1,2},{2,3},{3,4},{4,5},{5,6},{6,7},{7,8},{8,9},{9,10},{10,1... | collective-permute-start | bytes 24584 | tf_op jit(solution)/shard_map/ppermute | solution.py:16
  9.2 7.0 %collective-permute-start.1 = (f32[16,1,128]{2,1,0:T(1,128)S(1)}, f32[16,1,128]{2,1,0:T(1,128)S(1)}, u32[]{:S(2)}, u32[]{:S(2)}) collective-permute-start(f32[16,1,128]{2,1,0:T(1,128)S(1)} %get-tuple-element.510), channel_id=1, source_target_pairs={{1,0},{2,1},{3,2},{4,3},{5,4},{6,5},{7,6},{8,7},{9,8},{10,9},{11,1... | collective-permute-start | bytes 24584 | tf_op jit(solution)/shard_map/ppermute | solution.py:17
  11.4 4.8 %copy-start.3 = (f32[16,128,128]{2,1,0:T(8,128)S(1)}, f32[16,128,128]{2,1,0:T(8,128)}, u32[]{:S(2)}) copy-start(f32[16,128,128]{2,1,0:T(8,128)} %param.10) | copy-start | bytes 3145732
  16.2 1.3 copy-start.1
  16.2 1.9 copy-start.2
  16.5 1.0 copy-start
  84.5 9.4 %collective-permute-start.2 = (f32[4,128,128]{2,1,0:T(8,128)S(1)}, f32[4,128,128]{2,1,0:T(8,128)S(1)}, u32[]{:S(2)}, u32[]{:S(2)}) collective-permute-start(f32[4,128,128]{2,1,0:T(8,128)S(1)} %pad_maximum_fusion.4), channel_id=1, source_target_pairs={{16,0},{32,16},{48,32},{64,48},{80,64},{96,80},{112,96},{128,112},... | collective-permute-start | bytes 786440 | tf_op jit(solution)/shard_map/ppermute | solution.py:25
  241.2 8.3 %collective-permute-start.3 = (f32[128,128]{1,0:T(8,128)S(1)}, f32[128,128]{1,0:T(8,128)S(1)}, u32[]{:S(2)}, u32[]{:S(2)}) collective-permute-start(f32[128,128]{1,0:T(8,128)S(1)} %get-tuple-element.507), channel_id=1, source_target_pairs={{0,16},{16,32},{32,48},{48,64},{64,80},{80,96},{96,112},{112,128},... | collective-permute-start | bytes 196616 | tf_op jit(solution)/shard_map/ppermute | solution.py:25
Sparse Core Ops, SparseCore 0:
  95.7 63.7 all-gather.2
where the time goes:
time: 262 us; the launch traced here: 258 us
  other arithmetic  131 us (50%)
  waiting for transfers between devices  74.8 us (29%)
  local copies, waits for them, and re-layouts  27.8 us (11%)
  between operations  13.6 us (5%)
  starting transfers between devices  9.76 us (4%)
    dynamic_update_slice x93, other arithmetic, many_solve(): lax.scan(forward, start, (diag_part, lower_part, upper_part, sources))  124 us
    all_gather x1, waiting for transfers between devices, body(): gathered = lax.all_gather(bundle, 'gx', axis=0, tiled=True)  63.9 us
    mul x15, local copies, waits for them, and re-layouts, backward(): result = value_row - ratio_row[None] * later_value  12.7 us
    ppermute x2, waiting for transfers between devices, shifted(): lax.ppermute(value, axis, [(source, source + steps) for source in range(i...  10.9 us
    ppermute x2, starting transfers between devices, shifted(): lax.ppermute(value, axis, [(source, source + steps) for source in range(i...  6.73 us
  transfers between devices with their start and end apart: 5, of which 3 were waited for; matrix products, arithmetic and copies ran while one was open for 2% of the time, Pallas kernels for 0%

commit v1 on v0

v1 whole, which is shorter than its diff:
```python
import jax
import jax.numpy as jnp
from jax import lax
from jax.sharding import PartitionSpec as P

y_weight = 0.15


def with_halo(shard, sides, width):
    for axis, dim in sides:
        size, length = (lax.axis_size(axis), shard.shape[dim])
        up = [(i, (i + 1) % size) for i in range(size - 1)]
        down = [(j, i) for i, j in up]
        last = lax.slice_in_dim(shard, length - width, length, axis=dim)
        initial = lax.slice_in_dim(shard, 0, width, axis=dim)
        before = lax.ppermute(last, axis, up)
        after = lax.ppermute(initial, axis, down)
        shard = jnp.concatenate([before, shard, after], axis=dim)
    return shard


def local_solve(coupling, source_term):
    height = coupling.shape[0]
    n = height - 1
    ratios, v_loc, v_left = [], [], []
    for r in range(n):
        diag = 1.0 + coupling[r] + coupling[r + 1]
        lower = -coupling[r]
        upper = -coupling[r + 1]
        if r == 0:
            denom = diag
            loc = source_term[0] / denom
            left = coupling[0] / denom
        else:
            denom = diag - lower * ratios[-1]
            loc = (source_term[r] - lower * v_loc[-1]) / denom
            left = (-lower * v_left[-1]) / denom
        ratios.append(upper / denom)
        v_loc.append(loc)
        v_left.append(left)
    right_last = coupling[n] / denom
    s_loc = [None] * n
    s_left = [None] * n
    s_right = [None] * n
    s_loc[n - 1] = v_loc[n - 1]
    s_left[n - 1] = v_left[n - 1]
    s_right[n - 1] = right_last
    for r in range(n - 2, -1, -1):
        s_loc[r] = v_loc[r] - ratios[r] * s_loc[r + 1]
        s_left[r] = v_left[r] - ratios[r] * s_left[r + 1]
        s_right[r] = -(ratios[r] * s_right[r + 1])
    return s_loc, s_left, s_right


def reduced_solve(lower, middle, upper, target):
    count = len(middle)
    ratios, values = [], []
    for p in range(count):
        if p == 0:
            denom = middle[0]
            value = target[0] / denom
        else:
            denom = middle[p] - lower[p] * ratios[-1]
            value = (target[p] - lower[p] * values[-1]) / denom
        ratios.append(upper[p] / denom)
        values.append(value)
    solved = [None] * count
    solved[count - 1] = values[count - 1]
    for p in range(count - 2, -1, -1):
        solved[p] = values[p] - ratios[p] * solved[p + 1]
    return solved


def body(energy, coupling):
    height, width, depth = energy.shape
    padded = with_halo(energy, (("gy", 1),), 1)
    source_term = energy + y_weight * (padded[:, :-2] - 2.0 * energy + padded[:, 2:])
    s_loc, s_left, s_right = local_solve(coupling, source_term)
    n = height - 1
    position = lax.axis_index("gx")
    own_face = coupling[height - 1]
    lower_own = jnp.where(position == 0, 0.0, -own_face * s_left[n - 1])
    middle_own = 1.0 + own_face - own_face * s_right[n - 1]
    target_own = source_term[height - 1] + own_face * s_loc[n - 1]
    face = coupling[0]
    middle_next = face - face * s_left[0]
    upper_prev = -face * s_right[0]
    target_next = face * s_loc[0]
    parts = lax.axis_size("gx")
    chunk = width // parts
    pack = jnp.stack([lower_own, middle_own, target_own, middle_next, upper_prev, target_next], 0)
    pack = pack.reshape(6, parts, chunk, depth)
    got = lax.all_to_all(pack, "gx", 1, 1, tiled=True)
    lower = [got[0, p] for p in range(parts)]
    middle = [got[1, p] + got[3, p + 1] if p + 1 < parts else got[1, p] for p in range(parts)]
    upper = [got[4, p + 1] if p + 1 < parts else jnp.zeros_like(got[4, p]) for p in range(parts)]
    target = [got[2, p] + got[5, p + 1] if p + 1 < parts else got[2, p] for p in range(parts)]
    solved = reduced_solve(lower, middle, upper, target)
    own = jnp.stack(solved, 0)
    prev = jnp.stack([jnp.zeros_like(solved[0])] + solved[:-1], 0)
    back = jnp.stack([own, prev], 0)
    back = lax.all_to_all(back, "gx", 1, 1, tiled=True)
    last_value = back[0].reshape(width, depth)
    previous = back[1].reshape(width, depth)
    rows = [s_loc[r] + s_left[r] * previous + s_right[r] * last_value for r in range(n)]
    rows.append(last_value)
    return jnp.stack(rows, 0)


def solution(mesh):
    in_specs = (P("gx", "gy", None), P("gx", "gy", None))
    out_specs = P("gx", "gy", None)
    return jax.shard_map(body, mesh=mesh, in_specs=in_specs, out_specs=out_specs, check_vma=False)
```

time: 262 us -> 42.8 us (0.16)
  the two profiles are of different devices: /device:TPU:8 before, /device:TPU:32 now
where the time goes in v1:
time: 42.8 us; the launch traced here: 42.5 us
  starting transfers between devices  12.6 us (29%)
  waiting for transfers between devices  11.4 us (27%)
  blocking collectives  11.2 us (26%)
  other arithmetic  3.66 us (9%)
  local copies, waits for them, and re-layouts  3.38 us (8%)
    all_to_all x1, waiting for transfers between devices, body(): got = lax.all_to_all(pack, 'gx', 1, 1, tiled=True)  11.4 us
    all_to_all x1, blocking collectives, body(): back = lax.all_to_all(back, 'gx', 1, 1, tiled=True)  11.2 us
    all_to_all x1, starting transfers between devices, body(): got = lax.all_to_all(pack, 'gx', 1, 1, tiled=True)  7.03 us
    ppermute x1, starting transfers between devices, with_halo(): after = lax.ppermute(initial, axis, down)  3.64 us
    unnamed x22, other arithmetic  3.01 us
    ppermute x1, starting transfers between devices, with_halo(): before = lax.ppermute(last, axis, up)  1.92 us
    unnamed x23, local copies, waits for them, and re-layouts  1.84 us
    slice x1, local copies, waits for them, and re-layouts, with_halo(): last = lax.slice_in_dim(shard, length - width, length, axis=dim)  0.88 us
  transfers between devices with their start and end apart: 3, of which 1 were waited for; matrix products, arithmetic and copies ran while one was open for 4% of the time, Pallas kernels for 0%

profile of v1, /device:TPU:32, one launch (start us, length us, event | category | flops | bytes accessed | tf_op | source)
XLA Modules:
  0.0 42.5 jit_solution(8499277171414437597)
XLA Ops:
  0.0 0.9 %fusion.185 = (f32[16,1,128]{2,1,0:T(1,128)S(1)}, f32[16,1,128]{2,1,0:T(1,128)S(1)}) fusion(f32[16,128,128]{2,1,0:T(8,128)} %param.2), kind=kLoop, calls=%fused_computation.410 | loop fusion | bytes 32768 | tf_op jit(solution)/shard_map/slice | solution.py:14
  0.9 1.9 %collective-permute-start = (f32[16,1,128]{2,1,0:T(1,128)S(1)}, f32[16,1,128]{2,1,0:T(1,128)S(1)}, u32[]{:S(2)}, u32[]{:S(2)}) collective-permute-start(f32[16,1,128]{2,1,0:T(1,128)S(1)} %get-tuple-element.129), channel_id=1, source_target_pairs={{0,1},{1,2},{2,3},{3,4},{4,5},{5,6},{6,7},{7,8},{8,9},{9,10},{10,1... | collective-permute-start | bytes 24584 | tf_op jit(solution)/shard_map/ppermute | solution.py:16
  2.8 3.6 %collective-permute-start.1 = (f32[16,1,128]{2,1,0:T(1,128)S(1)}, f32[16,1,128]{2,1,0:T(1,128)S(1)}, u32[]{:S(2)}, u32[]{:S(2)}) collective-permute-start(f32[16,1,128]{2,1,0:T(1,128)S(1)} %get-tuple-element.130), channel_id=1, source_target_pairs={{1,0},{2,1},{3,2},{4,3},{5,4},{6,5},{7,6},{8,7},{9,8},{10,9},{11,1... | collective-permute-start | bytes 24584 | tf_op jit(solution)/shard_map/ppermute | solution.py:17
  6.5 0.0 copy-start
  6.5 0.0 copy-start.1
  6.5 1.8 %constant_dynamic-update-slice_fusion.5 = (f32[6,16,8,128]{3,2,0,1:T(8,128)S(1)}, f32[1,128,128]{2,1,0:T(8,128)S(1)}, f32[1,128,128]{2,1,0:T(8,128)S(1)}, f32[1,...) fusion(f32[16,128,128]{2,1,0:T(8,128)} %param.3, ...), kind=kLoop, calls=%fused_computation.12 | loop fusion | flops 1933311 | bytes 3538945
  8.3 0.0 collective-permute-done
  8.3 0.0 collective-permute-done.1
  8.3 0.1 copy-done.1
  8.4 0.3 fusion.2
  8.8 0.3 constant_dynamic-update-slice_fusion.3
  9.0 0.2 constant_dynamic-update-slice_fusion.2
  9.2 0.1 constant_dynamic-update-slice_fusion.1
  9.3 0.2 constant_dynamic-update-slice_fusion
  9.5 0.0 copy-start.2
  9.6 0.7 %copy-done.2 = f32[6,16,8,128]{3,2,0,1:T(8,128)} copy-done((f32[6,16,8,128]{3,2,0,1:T(8,128)}, f32[6,16,8,128]{3,2,0,1:T(8,128)S(1)}, u32[]{:S(2)}) %copy-start.2) | copy-done | bytes 393240
  10.3 7.0 %all-to-all-start = ((f32[6,16,8,128]{3,2,0,1:T(8,128)}), f32[6,16,8,128]{3,2,0,1:T(8,128)S(1)}, u32[]{:S(2)}, u32[]{:S(2)}) async-start(f32[6,16,8,128]{3,2,0,1:T(8,128)} %copy-done.2), calls=%async_computation | async-start | bytes 786432 | tf_op jit(solution)/shard_map/all_to_all | solution.py:93
  17.4 11.4 %all-to-all-done = f32[6,16,8,128]{3,2,0,1:T(8,128)S(1)} async-done(((f32[6,16,8,128]{3,2,0,1:T(8,128)}), f32[6,16,8,128]{3,2,0,1:T(8,128)S(1)}, u32[]{:S(2)}, u32[]{:S(2)}) %all-to-all-start) | async-done | bytes 393248 | tf_op jit(solution)/shard_map/all_to_all | solution.py:93
  28.7 0.1 fusion.30
  28.9 0.1 constant_dynamic-update-slice_fusion.21
  29.2 11.2 %all_to_all.10 = f32[2,16,8,128]{3,2,0,1:T(8,128)S(1)} all-to-all(f32[2,16,8,128]{3,2,0,1:T(8,128)S(1)} %copy.94), channel_id=1, replica_groups=mesh['gx'=16,'gy'=16] {'gx'}, dimensions={1} | all-to-all | bytes 262144 | tf_op jit(solution)/shard_map/all_to_all | solution.py:102
  40.9 0.0 copy-start.3
  40.9 1.0 %copy-done.3 = f32[16,128,128]{2,1,0:T(8,128)} copy-done((f32[16,128,128]{2,1,0:T(8,128)}, f32[16,128,128]{2,1,0:T(8,128)S(1)}, u32[]{:S(2)}) %copy-start.3) | copy-done | bytes 1048600
  41.8 0.6 %constant_dynamic-update-slice_fusion.38 = f32[16,128,128]{2,1,0:T(8,128)} fusion(f32[16,128,128]{2,1,0:T(8,128)} %copy-done.3, f32[2,16,8,128]{3,2,0,1:T(8,128)S(1)} %all_to_all.10), kind=kLoop, calls=%fused_computation.45 | loop fusion | bytes 131072 | tf_op jit(solution)/shard_map/stack | solution.py:107
  (36 shorter events, 0.6 us)
Async XLA Ops:
  0.9 7.4 %collective-permute-start = (f32[16,1,128]{2,1,0:T(1,128)S(1)}, f32[16,1,128]{2,1,0:T(1,128)S(1)}, u32[]{:S(2)}, u32[]{:S(2)}) collective-permute-start(f32[16,1,128]{2,1,0:T(1,128)S(1)} %get-tuple-element.129), channel_id=1, source_target_pairs={{0,1},{1,2},{2,3},{3,4},{4,5},{5,6},{6,7},{7,8},{8,9},{9,10},{10,1... | collective-permute-start | bytes 24584 | tf_op jit(solution)/shard_map/ppermute | solution.py:16
  2.8 5.5 %collective-permute-start.1 = (f32[16,1,128]{2,1,0:T(1,128)S(1)}, f32[16,1,128]{2,1,0:T(1,128)S(1)}, u32[]{:S(2)}, u32[]{:S(2)}) collective-permute-start(f32[16,1,128]{2,1,0:T(1,128)S(1)} %get-tuple-element.130), channel_id=1, source_target_pairs={{1,0},{2,1},{3,2},{4,3},{5,4},{6,5},{7,6},{8,7},{9,8},{10,9},{11,1... | collective-permute-start | bytes 24584 | tf_op jit(solution)/shard_map/ppermute | solution.py:17
  6.5 1.8 %copy-start = (f32[16,128,128]{2,1,0:T(8,128)S(1)}, f32[16,128,128]{2,1,0:T(8,128)}, u32[]{:S(2)}) copy-start(f32[16,128,128]{2,1,0:T(8,128)} %param.3) | copy-start | bytes 3145732
  6.5 1.9 %copy-start.1 = (f32[16,128,128]{2,1,0:T(8,128)S(1)}, f32[16,128,128]{2,1,0:T(8,128)}, u32[]{:S(2)}) copy-start(f32[16,128,128]{2,1,0:T(8,128)} %param.2) | copy-start | bytes 3145732
  9.5 0.7 %copy-start.2 = (f32[6,16,8,128]{3,2,0,1:T(8,128)}, f32[6,16,8,128]{3,2,0,1:T(8,128)S(1)}, u32[]{:S(2)}) copy-start(f32[6,16,8,128]{3,2,0,1:T(8,128)S(1)} %get-tuple-element.51) | copy-start | bytes 1179652
  10.3 18.4 %all-to-all-start = ((f32[6,16,8,128]{3,2,0,1:T(8,128)}), f32[6,16,8,128]{3,2,0,1:T(8,128)S(1)}, u32[]{:S(2)}, u32[]{:S(2)}) async-start(f32[6,16,8,128]{3,2,0,1:T(8,128)} %copy-done.2), calls=%async_computation | async-start | bytes 786432 | tf_op jit(solution)/shard_map/all_to_all | solution.py:93
  40.9 1.0 %copy-start.3 = (f32[16,128,128]{2,1,0:T(8,128)}, f32[16,128,128]{2,1,0:T(8,128)S(1)}, u32[]{:S(2)}) copy-start(f32[16,128,128]{2,1,0:T(8,128)S(1)} %constant_dynamic-update-slice_fusion.39) | copy-start | bytes 3145732

commit v2 on v1

v2 whole, which is shorter than its diff:
```python
import jax
import jax.numpy as jnp
from jax import lax
from jax.sharding import PartitionSpec as P
from jax.experimental import pallas as pl
from jax.experimental.pallas import tpu as pltpu
import os

y_weight = 0.15
tile = 8
block = 32
interpret = bool(os.environ.get("SOL_INTERPRET"))


def with_halo(shard, sides, width):
    for axis, dim in sides:
        size, length = (lax.axis_size(axis), shard.shape[dim])
        up = [(i, (i + 1) % size) for i in range(size - 1)]
        down = [(j, i) for i, j in up]
        last = lax.slice_in_dim(shard, length - width, length, axis=dim)
        initial = lax.slice_in_dim(shard, 0, width, axis=dim)
        before = lax.ppermute(last, axis, up)
        after = lax.ppermute(initial, axis, down)
        shard = jnp.concatenate([before, shard, after], axis=dim)
    return shard


def reduced_solve(lower, middle, upper, target):
    count = len(middle)
    ratios, values = [], []
    for p in range(count):
        if p == 0:
            denom = middle[0]
            value = target[0] / denom
        else:
            denom = middle[p] - lower[p] * ratios[-1]
            value = (target[p] - lower[p] * values[-1]) / denom
        ratios.append(upper[p] / denom)
        values.append(value)
    solved = [None] * count
    solved[count - 1] = values[count - 1]
    for p in range(count - 2, -1, -1):
        solved[p] = values[p] - ratios[p] * solved[p + 1]
    return solved


def forward_rows(c, s, first_extra=None, last_extra=None):
    n = len(c) - 1
    ratios, values, lefts, denom = [], [], [], None
    for r in range(n):
        diag = 1.0 + c[r] + c[r + 1]
        lower = -c[r]
        upper = -c[r + 1]
        src = s[r]
        if r == 0 and first_extra is not None:
            src = src + first_extra
        if r == n - 1 and last_extra is not None:
            src = src + last_extra
        if r == 0:
            denom = diag
            value = src / denom
            left = c[0] / denom
        else:
            denom = diag - lower * ratios[-1]
            value = (src - lower * values[-1]) / denom
            left = (-lower * lefts[-1]) / denom
        ratios.append(upper / denom)
        values.append(value)
        lefts.append(left)
    return ratios, values, lefts, denom


def pack_kernel(pos_ref, c_ref, s_ref, out_ref):
    height = c_ref.shape[0]
    n = height - 1
    first = pos_ref[0] == 0

    def step(q, carry):
        rows = pl.ds(pl.multiple_of(q * tile, tile), tile)
        c = [c_ref[r, rows, :] for r in range(height)]
        s = [s_ref[r, rows, :] for r in range(height)]
        ratios, values, lefts, denom = forward_rows(c, s)
        right = c[n] / denom
        s_loc, s_left, s_right = values[n - 1], lefts[n - 1], right
        own_face = c[n]
        lower_own = jnp.where(first, 0.0, -own_face * s_left)
        middle_own = 1.0 + own_face - own_face * s_right
        target_own = s[n] + own_face * s_loc
        for r in range(n - 2, -1, -1):
            s_loc = values[r] - ratios[r] * s_loc
            s_left = lefts[r] - ratios[r] * s_left
            s_right = -(ratios[r] * s_right)
        face = c[0]
        pieces = [lower_own, middle_own, target_own, face - face * s_left, -face * s_right, face * s_loc]
        for i, piece in enumerate(pieces):
            out_ref[q, i] = piece
        return carry

    lax.fori_loop(0, c_ref.shape[1] // tile, step, 0)


def finish_kernel(c_ref, s_ref, x_ref, out_ref):
    height = c_ref.shape[0]
    n = height - 1

    def step(q, carry):
        rows = pl.ds(pl.multiple_of(q * tile, tile), tile)
        c = [c_ref[r, rows, :] for r in range(height)]
        s = [s_ref[r, rows, :] for r in range(height)]
        last_value = x_ref[q, 0]
        previous = x_ref[q, 1]
        ratios, values, _, _ = forward_rows(c, s, c[0] * previous, c[n] * last_value)
        u = values[n - 1]
        out_ref[n - 1, rows, :] = u
        for r in range(n - 2, -1, -1):
            u = values[r] - ratios[r] * u
            out_ref[r, rows, :] = u
        out_ref[n, rows, :] = last_value
        return carry

    lax.fori_loop(0, c_ref.shape[1] // tile, step, 0)


def local_pack(position, coupling, source_term):
    height, width, depth = coupling.shape
    grid = (width // block,)
    full = pl.BlockSpec((height, block, depth), lambda g: (0, g, 0))
    per = block // tile
    return pl.pallas_call(
        pack_kernel,
        grid=grid,
        in_specs=[pl.BlockSpec(memory_space=pltpu.SMEM), full, full],
        out_specs=pl.BlockSpec((per, 6, tile, depth), lambda g: (g, 0, 0, 0)),
        out_shape=jax.ShapeDtypeStruct((width // tile, 6, tile, depth), jnp.float32),
        interpret=interpret,
    )(position, coupling, source_term)


def finish(coupling, source_term, solved):
    height, width, depth = coupling.shape
    grid = (width // block,)
    full = pl.BlockSpec((height, block, depth), lambda g: (0, g, 0))
    per = block // tile
    return pl.pallas_call(
        finish_kernel,
        grid=grid,
        in_specs=[full, full, pl.BlockSpec((per, 2, tile, depth), lambda g: (g, 0, 0, 0))],
        out_specs=full,
        out_shape=jax.ShapeDtypeStruct((height, width, depth), jnp.float32),
        interpret=interpret,
    )(coupling, source_term, solved)


def body(energy, coupling):
    height, width, depth = energy.shape
    padded = with_halo(energy, (("gy", 1),), 1)
    source_term = energy + y_weight * (padded[:, :-2] - 2.0 * energy + padded[:, 2:])
    position = lax.axis_index("gx").astype(jnp.int32).reshape(1)
    parts = lax.axis_size("gx")
    chunk = width // parts
    pack = local_pack(position, coupling, source_term)
    pack = pack.reshape(parts, chunk // tile, 6, tile, depth).transpose(2, 0, 1, 3, 4)
    pack = pack.reshape(6, parts, chunk, depth)
    got = lax.all_to_all(pack, "gx", 1, 1, tiled=True)
    lower = [got[0, p] for p in range(parts)]
    middle = [got[1, p] + got[3, p + 1] if p + 1 < parts else got[1, p] for p in range(parts)]
    upper = [got[4, p + 1] if p + 1 < parts else jnp.zeros_like(got[4, p]) for p in range(parts)]
    target = [got[2, p] + got[5, p + 1] if p + 1 < parts else got[2, p] for p in range(parts)]
    solved = reduced_solve(lower, middle, upper, target)
    own = jnp.stack(solved, 0)
    prev = jnp.stack([jnp.zeros_like(solved[0])] + solved[:-1], 0)
    back = jnp.stack([own, prev], 0)
    back = lax.all_to_all(back, "gx", 1, 1, tiled=True)
    back = back.reshape(2, width // tile, tile, depth).transpose(1, 0, 2, 3)
    return finish(coupling, source_term, back)


def solution(mesh):
    in_specs = (P("gx", "gy", None), P("gx", "gy", None))
    out_specs = P("gx", "gy", None)
    return jax.shard_map(body, mesh=mesh, in_specs=in_specs, out_specs=out_specs, check_vma=False)
```

time: 42.8 us -> 52 us (1.21)
  the two profiles are of different devices: /device:TPU:32 before, /device:TPU:1 now
where the time goes in v2:
time: 52 us; the launch traced here: 51.6 us
  starting transfers between devices  13.6 us (26%)
  waiting for transfers between devices  12.2 us (23%)
  blocking collectives  11.1 us (21%)
  Pallas kernels  9.76 us (19%)
  other arithmetic  3.75 us (7%)
  local copies, waits for them, and re-layouts  0.94 us (2%)
    all_to_all x1, blocking collectives, body(): back = lax.all_to_all(back, 'gx', 1, 1, tiled=True)  11.1 us
    all_to_all x1, waiting for transfers between devices, body(): got = lax.all_to_all(pack, 'gx', 1, 1, tiled=True)  9.19 us
    all_to_all x1, starting transfers between devices, body(): got = lax.all_to_all(pack, 'gx', 1, 1, tiled=True)  6.75 us
    pallas_call x1, Pallas kernels, finish(): pl.pallas_call(finish_kernel, grid=grid, in_specs=[full, full, pl.BlockSp...  4.92 us
    ppermute x1, starting transfers between devices, with_halo(): before = lax.ppermute(last, axis, up)  4.92 us
    pallas_call x1, Pallas kernels, local_pack(): pl.pallas_call(pack_kernel, grid=grid, in_specs=[pl.BlockSpec(memory_spac...  4.83 us
    add x1, other arithmetic, body(): energy + y_weight * (padded[:, :-2] - 2.0 * energy + padded[:, 2:])  3.55 us
    ppermute x1, waiting for transfers between devices, with_halo(): after = lax.ppermute(initial, axis, down)  3.03 us
  transfers between devices with their start and end apart: 3, of which 2 were waited for; matrix products, arithmetic and copies ran while one was open for 0% of the time, Pallas kernels for 0%

profile of v2, /device:TPU:1, one launch (start us, length us, event | category | flops | bytes accessed | tf_op | source)
XLA Modules:
  0.0 51.6 jit_solution(4780542796183105230)
XLA Ops:
  0.0 0.9 %fusion.155 = (f32[16,1,128]{2,1,0:T(1,128)S(1)}, f32[16,1,128]{2,1,0:T(1,128)S(1)}) fusion(f32[16,128,128]{2,1,0:T(8,128)} %param.2), kind=kLoop, calls=%fused_computation.267 | loop fusion | bytes 32768 | tf_op jit(solution)/shard_map/slice | solution.py:20
  0.9 4.9 %collective-permute-start = (f32[16,1,128]{2,1,0:T(1,128)S(1)}, f32[16,1,128]{2,1,0:T(1,128)S(1)}, u32[]{:S(2)}, u32[]{:S(2)}) collective-permute-start(f32[16,1,128]{2,1,0:T(1,128)S(1)} %get-tuple-element.51), channel_id=1, source_target_pairs={{0,1},{1,2},{2,3},{3,4},{4,5},{5,6},{6,7},{7,8},{8,9},{9,10},{10,1... | collective-permute-start | bytes 24584 | tf_op jit(solution)/shard_map/ppermute | solution.py:22
  5.8 1.9 %collective-permute-start.1 = (f32[16,1,128]{2,1,0:T(1,128)S(1)}, f32[16,1,128]{2,1,0:T(1,128)S(1)}, u32[]{:S(2)}, u32[]{:S(2)}) collective-permute-start(f32[16,1,128]{2,1,0:T(1,128)S(1)} %get-tuple-element.52), channel_id=1, source_target_pairs={{1,0},{2,1},{3,2},{4,3},{5,4},{6,5},{7,6},{8,7},{9,8},{10,9},{11,1... | collective-permute-start | bytes 24584 | tf_op jit(solution)/shard_map/ppermute | solution.py:23
  7.8 0.0 collective-permute-done
  7.8 3.0 %collective-permute-done.1 = f32[16,1,128]{2,1,0:T(1,128)S(1)} collective-permute-done((f32[16,1,128]{2,1,0:T(1,128)S(1)}, f32[16,1,128]{2,1,0:T(1,128)S(1)}, u32[]{:S(2)}, u32[]{:S(2)}) %collective-permute-start.1) | collective-permute-done | bytes 8224 | tf_op jit(solution)/shard_map/ppermute | solution.py:23
  10.8 3.5 %fusion.2.s_ref = f32[16,128,128]{2,1,0:T(8,128)} fusion(f32[16,128,128]{2,1,0:T(8,128)} %param.2, f32[16,1,128]{2,1,0:T(1,128)S(1)} %collective-permute-done.1, f32[16,1,128]{2,1,0:T(1,128)S(1)} %collective-permute-done), kind=kLoop, calls=%fused_computation.3 | loop fusion | flops 1835008 | bytes 2113536 | tf_op jit(solution)/shard_map/add | solution.py:157
  14.3 4.8 %shard_map.28 = f32[16,6,8,128]{3,2,1,0:T(8,128)} custom-call(s32[1]{0:T(128)} %bitcast.pos_ref, f32[16,128,128]{2,1,0:T(8,128)} %c_ref.3, f32[16,128,128]{2,1,0:T(8,128)} %fusion.2.s_ref), custom_call_target="tpu_custom_call" | custom-call | tf_op jit(solution)/shard_map/pallas_call | solution.py:129
  19.2 6.8 %all-to-all-start = ((f32[6,16,8,128]{3,2,0,1:T(8,128)}), f32[6,16,8,128]{3,2,0,1:T(8,128)S(1)}, u32[]{:S(2)}, u32[]{:S(2)}) async-start(f32[6,16,8,128]{3,2,0,1:T(8,128)} %bitcast.975), calls=%async_computation | async-start | bytes 786432 | tf_op jit(solution)/shard_map/all_to_all | solution.py:164
  25.9 9.2 %all-to-all-done = f32[6,16,8,128]{3,2,0,1:T(8,128)S(1)} async-done(((f32[6,16,8,128]{3,2,0,1:T(8,128)}), f32[6,16,8,128]{3,2,0,1:T(8,128)S(1)}, u32[]{:S(2)}, u32[]{:S(2)}) %all-to-all-start) | async-done | bytes 393248 | tf_op jit(solution)/shard_map/all_to_all | solution.py:164
  35.1 0.1 fusion.14
  35.2 0.1 constant_dynamic-update-slice_fusion.15
  35.5 11.1 %all_to_all.10 = f32[2,16,8,128]{3,2,0,1:T(8,128)} all-to-all(f32[2,16,8,128]{3,2,0,1:T(8,128)S(1)} %pad_maximum_fusion.2), channel_id=1, replica_groups=mesh['gx'=16,'gy'=16] {'gx'}, dimensions={1} | all-to-all | bytes 262144 | tf_op jit(solution)/shard_map/all_to_all | solution.py:173
  46.6 4.9 %shard_map.29 = f32[16,128,128]{2,1,0:T(8,128)} custom-call(f32[16,128,128]{2,1,0:T(8,128)} %c_ref.3, f32[16,128,128]{2,1,0:T(8,128)} %fusion.2.s_ref, f32[16,2,8,128]{3,2,1,0:T(8,128)} %bitcast.976), custom_call_target="tpu_custom_call" | custom-call | tf_op jit(solution)/shard_map/pallas_call | solution.py:144
  (18 shorter events, 0.1 us)
Async XLA Ops:
  0.9 6.9 %collective-permute-start = (f32[16,1,128]{2,1,0:T(1,128)S(1)}, f32[16,1,128]{2,1,0:T(1,128)S(1)}, u32[]{:S(2)}, u32[]{:S(2)}) collective-permute-start(f32[16,1,128]{2,1,0:T(1,128)S(1)} %get-tuple-element.51), channel_id=1, source_target_pairs={{0,1},{1,2},{2,3},{3,4},{4,5},{5,6},{6,7},{7,8},{8,9},{9,10},{10,1... | collective-permute-start | bytes 24584 | tf_op jit(solution)/shard_map/ppermute | solution.py:22
  5.8 5.0 %collective-permute-start.1 = (f32[16,1,128]{2,1,0:T(1,128)S(1)}, f32[16,1,128]{2,1,0:T(1,128)S(1)}, u32[]{:S(2)}, u32[]{:S(2)}) collective-permute-start(f32[16,1,128]{2,1,0:T(1,128)S(1)} %get-tuple-element.52), channel_id=1, source_target_pairs={{1,0},{2,1},{3,2},{4,3},{5,4},{6,5},{7,6},{8,7},{9,8},{10,9},{11,1... | collective-permute-start | bytes 24584 | tf_op jit(solution)/shard_map/ppermute | solution.py:23
  19.2 16.0 %all-to-all-start = ((f32[6,16,8,128]{3,2,0,1:T(8,128)}), f32[6,16,8,128]{3,2,0,1:T(8,128)S(1)}, u32[]{:S(2)}, u32[]{:S(2)}) async-start(f32[6,16,8,128]{3,2,0,1:T(8,128)} %bitcast.975), calls=%async_computation | async-start | bytes 786432 | tf_op jit(solution)/shard_map/all_to_all | solution.py:164

commit v3 on v1

--- a/solution.py
+++ b/solution.py
@@ -28,17 +28,17 @@
         lower = -coupling[r]
         upper = -coupling[r + 1]
         if r == 0:
-            denom = diag
-            loc = source_term[0] / denom
-            left = coupling[0] / denom
+            inv = 1.0 / diag
+            loc = source_term[0] * inv
+            left = coupling[0] * inv
         else:
-            denom = diag - lower * ratios[-1]
-            loc = (source_term[r] - lower * v_loc[-1]) / denom
-            left = (-lower * v_left[-1]) / denom
-        ratios.append(upper / denom)
+            inv = 1.0 / (diag - lower * ratios[-1])
+            loc = (source_term[r] - lower * v_loc[-1]) * inv
+            left = (-lower * v_left[-1]) * inv
+        ratios.append(upper * inv)
         v_loc.append(loc)
         v_left.append(left)
-    right_last = coupling[n] / denom
+    right_last = coupling[n] * inv
     s_loc = [None] * n
     s_left = [None] * n
     s_right = [None] * n
@@ -57,12 +57,12 @@
     ratios, values = [], []
     for p in range(count):
         if p == 0:
-            denom = middle[0]
-            value = target[0] / denom
+            inv = 1.0 / middle[0]
+            value = target[0] * inv
         else:
-            denom = middle[p] - lower[p] * ratios[-1]
-            value = (target[p] - lower[p] * values[-1]) / denom
-        ratios.append(upper[p] / denom)
+            inv = 1.0 / (middle[p] - lower[p] * ratios[-1])
+            value = (target[p] - lower[p] * values[-1]) * inv
+        ratios.append(upper[p] * inv)
         values.append(value)
     solved = [None] * count
     solved[count - 1] = values[count - 1]

time: 42.8 us -> 42.7 us (level)
    unnamed x22 -> x21, other arithmetic: 3.01 us -> 2.96 us
    unnamed x23 -> x24, local copies, waits for them, and re-layouts: 1.84 us -> 1.85 us
where the time goes in v3:
time: 42.7 us; the launch traced here: 42.4 us
  starting transfers between devices  12.6 us (30%)
  waiting for transfers between devices  11.4 us (27%)
  blocking collectives  11.2 us (26%)
  other arithmetic  3.61 us (8%)
  local copies, waits for them, and re-layouts  3.39 us (8%)
    all_to_all x1, waiting for transfers between devices, body(): got = lax.all_to_all(pack, 'gx', 1, 1, tiled=True)  11.4 us
    all_to_all x1, blocking collectives, body(): back = lax.all_to_all(back, 'gx', 1, 1, tiled=True)  11.2 us
    all_to_all x1, starting transfers between devices, body(): got = lax.all_to_all(pack, 'gx', 1, 1, tiled=True)  7.03 us
    ppermute x1, starting transfers between devices, with_halo(): after = lax.ppermute(initial, axis, down)  3.64 us
    unnamed x21, other arithmetic  2.96 us
    ppermute x1, starting transfers between devices, with_halo(): before = lax.ppermute(last, axis, up)  1.92 us
    unnamed x24, local copies, waits for them, and re-layouts  1.85 us
    slice x1, local copies, waits for them, and re-layouts, with_halo(): last = lax.slice_in_dim(shard, length - width, length, axis=dim)  0.88 us
  transfers between devices with their start and end apart: 3, of which 1 were waited for; matrix products, arithmetic and copies ran while one was open for 4% of the time, Pallas kernels for 0%

profile of v3, /device:TPU:32, one launch (start us, length us, event | category | flops | bytes accessed | tf_op | source)
XLA Modules:
  0.0 42.4 jit_solution(7574459724299496804)
XLA Ops:
  0.0 0.9 %fusion.199 = (f32[16,1,128]{2,1,0:T(1,128)S(1)}, f32[16,1,128]{2,1,0:T(1,128)S(1)}) fusion(f32[16,128,128]{2,1,0:T(8,128)} %param.2), kind=kLoop, calls=%fused_computation.426 | loop fusion | bytes 32768 | tf_op jit(solution)/shard_map/slice | solution.py:14
  0.9 1.9 %collective-permute-start = (f32[16,1,128]{2,1,0:T(1,128)S(1)}, f32[16,1,128]{2,1,0:T(1,128)S(1)}, u32[]{:S(2)}, u32[]{:S(2)}) collective-permute-start(f32[16,1,128]{2,1,0:T(1,128)S(1)} %get-tuple-element.128), channel_id=1, source_target_pairs={{0,1},{1,2},{2,3},{3,4},{4,5},{5,6},{6,7},{7,8},{8,9},{9,10},{10,1... | collective-permute-start | bytes 24584 | tf_op jit(solution)/shard_map/ppermute | solution.py:16
  2.8 3.6 %collective-permute-start.1 = (f32[16,1,128]{2,1,0:T(1,128)S(1)}, f32[16,1,128]{2,1,0:T(1,128)S(1)}, u32[]{:S(2)}, u32[]{:S(2)}) collective-permute-start(f32[16,1,128]{2,1,0:T(1,128)S(1)} %get-tuple-element.129), channel_id=1, source_target_pairs={{1,0},{2,1},{3,2},{4,3},{5,4},{6,5},{7,6},{8,7},{9,8},{10,9},{11,1... | collective-permute-start | bytes 24584 | tf_op jit(solution)/shard_map/ppermute | solution.py:17
  6.5 0.0 copy-start
  6.5 0.0 copy-start.1
  6.5 1.8 %constant_dynamic-update-slice_fusion.5 = (f32[6,16,8,128]{3,2,0,1:T(8,128)S(1)}, f32[1,128,128]{2,1,0:T(8,128)S(1)}, f32[1,128,128]{2,1,0:T(8,128)S(1)}, f32[1,...) fusion(f32[16,128,128]{2,1,0:T(8,128)} %param.3, ...), kind=kLoop, calls=%fused_computation.12 | loop fusion | flops 2179071 | bytes 3538945
  8.3 0.0 collective-permute-done
  8.3 0.0 collective-permute-done.1
  8.3 0.1 copy-done.1
  8.4 0.3 fusion.2
  8.8 0.2 constant_dynamic-update-slice_fusion.3
  9.0 0.2 constant_dynamic-update-slice_fusion.2
  9.2 0.1 constant_dynamic-update-slice_fusion.1
  9.3 0.2 constant_dynamic-update-slice_fusion
  9.5 0.0 copy-start.2
  9.5 0.7 %copy-done.2 = f32[6,16,8,128]{3,2,0,1:T(8,128)} copy-done((f32[6,16,8,128]{3,2,0,1:T(8,128)}, f32[6,16,8,128]{3,2,0,1:T(8,128)S(1)}, u32[]{:S(2)}) %copy-start.2) | copy-done | bytes 393240
  10.3 7.0 %all-to-all-start = ((f32[6,16,8,128]{3,2,0,1:T(8,128)}), f32[6,16,8,128]{3,2,0,1:T(8,128)S(1)}, u32[]{:S(2)}, u32[]{:S(2)}) async-start(f32[6,16,8,128]{3,2,0,1:T(8,128)} %copy-done.2), calls=%async_computation | async-start | bytes 786432 | tf_op jit(solution)/shard_map/all_to_all | solution.py:93
  17.3 11.4 %all-to-all-done = f32[6,16,8,128]{3,2,0,1:T(8,128)S(1)} async-done(((f32[6,16,8,128]{3,2,0,1:T(8,128)}), f32[6,16,8,128]{3,2,0,1:T(8,128)S(1)}, u32[]{:S(2)}, u32[]{:S(2)}) %all-to-all-start) | async-done | bytes 393248 | tf_op jit(solution)/shard_map/all_to_all | solution.py:93
  28.7 0.1 fusion.32
  28.8 0.1 constant_dynamic-update-slice_fusion.21
  29.1 11.2 %all_to_all.10 = f32[2,16,8,128]{3,2,0,1:T(8,128)S(1)} all-to-all(f32[2,16,8,128]{3,2,0,1:T(8,128)S(1)} %copy.94), channel_id=1, replica_groups=mesh['gx'=16,'gy'=16] {'gx'}, dimensions={1} | all-to-all | bytes 262144 | tf_op jit(solution)/shard_map/all_to_all | solution.py:102
  40.8 0.0 copy-start.3
  40.8 1.0 %copy-done.3 = f32[16,128,128]{2,1,0:T(8,128)} copy-done((f32[16,128,128]{2,1,0:T(8,128)}, f32[16,128,128]{2,1,0:T(8,128)S(1)}, u32[]{:S(2)}) %copy-start.3) | copy-done | bytes 1048600
  41.8 0.6 %constant_dynamic-update-slice_fusion.38 = f32[16,128,128]{2,1,0:T(8,128)} fusion(f32[16,128,128]{2,1,0:T(8,128)} %copy-done.3, f32[2,16,8,128]{3,2,0,1:T(8,128)S(1)} %all_to_all.10), kind=kLoop, calls=%fused_computation.45 | loop fusion | bytes 131072 | tf_op jit(solution)/shard_map/stack | solution.py:107
  (36 shorter events, 0.6 us)
Async XLA Ops:
  0.9 7.4 %collective-permute-start = (f32[16,1,128]{2,1,0:T(1,128)S(1)}, f32[16,1,128]{2,1,0:T(1,128)S(1)}, u32[]{:S(2)}, u32[]{:S(2)}) collective-permute-start(f32[16,1,128]{2,1,0:T(1,128)S(1)} %get-tuple-element.128), channel_id=1, source_target_pairs={{0,1},{1,2},{2,3},{3,4},{4,5},{5,6},{6,7},{7,8},{8,9},{9,10},{10,1... | collective-permute-start | bytes 24584 | tf_op jit(solution)/shard_map/ppermute | solution.py:16
  2.8 5.5 %collective-permute-start.1 = (f32[16,1,128]{2,1,0:T(1,128)S(1)}, f32[16,1,128]{2,1,0:T(1,128)S(1)}, u32[]{:S(2)}, u32[]{:S(2)}) collective-permute-start(f32[16,1,128]{2,1,0:T(1,128)S(1)} %get-tuple-element.129), channel_id=1, source_target_pairs={{1,0},{2,1},{3,2},{4,3},{5,4},{6,5},{7,6},{8,7},{9,8},{10,9},{11,1... | collective-permute-start | bytes 24584 | tf_op jit(solution)/shard_map/ppermute | solution.py:17
  6.5 1.8 %copy-start = (f32[16,128,128]{2,1,0:T(8,128)S(1)}, f32[16,128,128]{2,1,0:T(8,128)}, u32[]{:S(2)}) copy-start(f32[16,128,128]{2,1,0:T(8,128)} %param.3) | copy-start | bytes 3145732
  6.5 1.9 %copy-start.1 = (f32[16,128,128]{2,1,0:T(8,128)S(1)}, f32[16,128,128]{2,1,0:T(8,128)}, u32[]{:S(2)}) copy-start(f32[16,128,128]{2,1,0:T(8,128)} %param.2) | copy-start | bytes 3145732
  9.5 0.7 %copy-start.2 = (f32[6,16,8,128]{3,2,0,1:T(8,128)}, f32[6,16,8,128]{3,2,0,1:T(8,128)S(1)}, u32[]{:S(2)}) copy-start(f32[6,16,8,128]{3,2,0,1:T(8,128)S(1)} %get-tuple-element.50) | copy-start | bytes 1179652
  10.3 18.4 %all-to-all-start = ((f32[6,16,8,128]{3,2,0,1:T(8,128)}), f32[6,16,8,128]{3,2,0,1:T(8,128)S(1)}, u32[]{:S(2)}, u32[]{:S(2)}) async-start(f32[6,16,8,128]{3,2,0,1:T(8,128)} %copy-done.2), calls=%async_computation | async-start | bytes 786432 | tf_op jit(solution)/shard_map/all_to_all | solution.py:93
  40.8 1.0 %copy-start.3 = (f32[16,128,128]{2,1,0:T(8,128)}, f32[16,128,128]{2,1,0:T(8,128)S(1)}, u32[]{:S(2)}) copy-start(f32[16,128,128]{2,1,0:T(8,128)S(1)} %constant_dynamic-update-slice_fusion.39) | copy-start | bytes 3145732

commit v4 on v3

--- a/solution.py
+++ b/solution.py
@@ -62,7 +62,8 @@
         else:
             inv = 1.0 / (middle[p] - lower[p] * ratios[-1])
             value = (target[p] - lower[p] * values[-1]) * inv
-        ratios.append(upper[p] * inv)
+        if p + 1 < count:
+            ratios.append(upper[p] * inv)
         values.append(value)
     solved = [None] * count
     solved[count - 1] = values[count - 1]
@@ -93,11 +94,11 @@
     got = lax.all_to_all(pack, "gx", 1, 1, tiled=True)
     lower = [got[0, p] for p in range(parts)]
     middle = [got[1, p] + got[3, p + 1] if p + 1 < parts else got[1, p] for p in range(parts)]
-    upper = [got[4, p + 1] if p + 1 < parts else jnp.zeros_like(got[4, p]) for p in range(parts)]
+    upper = [got[4, p + 1] for p in range(parts - 1)]
     target = [got[2, p] + got[5, p + 1] if p + 1 < parts else got[2, p] for p in range(parts)]
     solved = reduced_solve(lower, middle, upper, target)
     own = jnp.stack(solved, 0)
-    prev = jnp.stack([jnp.zeros_like(solved[0])] + solved[:-1], 0)
+    prev = jnp.stack([solved[0] * 0.0] + solved[:-1], 0)
     back = jnp.stack([own, prev], 0)
     back = lax.all_to_all(back, "gx", 1, 1, tiled=True)
     last_value = back[0].reshape(width, depth)

time: 42.7 us -> 41.6 us (0.974)
  blocking collectives: 11.2 us -> 29.4 us
  waiting for transfers between devices: 11.4 us -> 0.01 us
  starting transfers between devices: 12.6 us -> 5.56 us
  local copies, waits for them, and re-layouts: 3.39 us -> 2.64 us
    all_to_all x0 -> x1, blocking collectives: none -> 18.2 us  [body(): got = lax.all_to_all(pack, 'gx', 1, 1, tiled=True)]
    all_to_all x1 -> x0, waiting for transfers between devices: 11.4 us -> none  [body(): got = lax.all_to_all(pack, 'gx', 1, 1, tiled=True)]
    all_to_all x1 -> x0, starting transfers between devices: 7.03 us -> none  [body(): got = lax.all_to_all(pack, 'gx', 1, 1, tiled=True)]
    unnamed x24 -> x21, local copies, waits for them, and re-layouts: 1.85 us -> 1.11 us
    unnamed x21 -> x22, other arithmetic: 2.96 us -> 2.88 us
  transfers between devices with their start and end apart: 3 -> 2, of which waited for: 1 -> 0; matrix products, arithmetic and copies ran while one was open for 4% -> 4% of each run, Pallas kernels for 0% -> 0%
where the time goes in v4:
time: 41.6 us; the launch traced here: 41.4 us
  blocking collectives  29.4 us (71%)
  starting transfers between devices  5.56 us (13%)
  other arithmetic  3.48 us (8%)
  local copies, waits for them, and re-layouts  2.64 us (6%)
    all_to_all x1, blocking collectives, body(): got = lax.all_to_all(pack, 'gx', 1, 1, tiled=True)  18.2 us
    all_to_all x1, blocking collectives, body(): back = lax.all_to_all(back, 'gx', 1, 1, tiled=True)  11.2 us
    ppermute x1, starting transfers between devices, with_halo(): after = lax.ppermute(initial, axis, down)  3.64 us
    unnamed x22, other arithmetic  2.88 us
    ppermute x1, starting transfers between devices, with_halo(): before = lax.ppermute(last, axis, up)  1.92 us
    unnamed x21, local copies, waits for them, and re-layouts  1.11 us
    slice x1, local copies, waits for them, and re-layouts, with_halo(): last = lax.slice_in_dim(shard, length - width, length, axis=dim)  0.88 us
  transfers between devices with their start and end apart: 2, of which 0 were waited for; matrix products, arithmetic and copies ran while one was open for 4% of the time, Pallas kernels for 0%

profile of v4, /device:TPU:32, one launch (start us, length us, event | category | flops | bytes accessed | tf_op | source)
XLA Modules:
  0.0 41.4 jit_solution(11507172757788315683)
XLA Ops:
  0.0 0.9 %fusion.199 = (f32[16,1,128]{2,1,0:T(1,128)S(1)}, f32[16,1,128]{2,1,0:T(1,128)S(1)}) fusion(f32[16,128,128]{2,1,0:T(8,128)} %param.2), kind=kLoop, calls=%fused_computation.426 | loop fusion | bytes 32768 | tf_op jit(solution)/shard_map/slice | solution.py:14
  0.9 1.9 %collective-permute-start = (f32[16,1,128]{2,1,0:T(1,128)S(1)}, f32[16,1,128]{2,1,0:T(1,128)S(1)}, u32[]{:S(2)}, u32[]{:S(2)}) collective-permute-start(f32[16,1,128]{2,1,0:T(1,128)S(1)} %get-tuple-element.128), channel_id=1, source_target_pairs={{0,1},{1,2},{2,3},{3,4},{4,5},{5,6},{6,7},{7,8},{8,9},{9,10},{10,1... | collective-permute-start | bytes 24584 | tf_op jit(solution)/shard_map/ppermute | solution.py:16
  2.8 3.6 %collective-permute-start.1 = (f32[16,1,128]{2,1,0:T(1,128)S(1)}, f32[16,1,128]{2,1,0:T(1,128)S(1)}, u32[]{:S(2)}, u32[]{:S(2)}) collective-permute-start(f32[16,1,128]{2,1,0:T(1,128)S(1)} %get-tuple-element.129), channel_id=1, source_target_pairs={{1,0},{2,1},{3,2},{4,3},{5,4},{6,5},{7,6},{8,7},{9,8},{10,9},{11,1... | collective-permute-start | bytes 24584 | tf_op jit(solution)/shard_map/ppermute | solution.py:17
  6.5 0.0 copy-start
  6.5 0.0 copy-start.1
  6.5 1.8 %constant_dynamic-update-slice_fusion.5 = (f32[6,16,8,128]{3,2,0,1:T(8,128)S(1)}, f32[1,128,128]{2,1,0:T(8,128)S(1)}, f32[1,128,128]{2,1,0:T(8,128)S(1)}, f32[1,...) fusion(f32[16,128,128]{2,1,0:T(8,128)} %param.3, ...), kind=kLoop, calls=%fused_computation.12 | loop fusion | flops 2179071 | bytes 3538945
  8.3 0.0 copy-done
  8.3 0.0 collective-permute-done
  8.3 0.0 collective-permute-done.1
  8.3 0.1 copy-done.1
  8.4 0.3 fusion.2
  8.8 0.2 constant_dynamic-update-slice_fusion.3
  9.0 0.2 constant_dynamic-update-slice_fusion.2
  9.1 0.1 constant_dynamic-update-slice_fusion.1
  9.2 0.2 constant_dynamic-update-slice_fusion
  9.4 18.2 %all_to_all.10 = f32[6,16,8,128]{3,2,0,1:T(8,128)S(1)} all-to-all(f32[6,16,8,128]{3,2,0,1:T(8,128)S(1)} %get-tuple-element.50), channel_id=1, replica_groups=mesh['gx'=16,'gy'=16] {'gx'}, dimensions={1} | all-to-all | bytes 786432 | tf_op jit(solution)/shard_map/all_to_all | solution.py:94
  27.6 0.1 fusion.32
  27.7 0.1 constant_dynamic-update-slice_fusion.21
  28.1 11.2 %all_to_all.11 = f32[2,16,8,128]{3,2,0,1:T(8,128)S(1)} all-to-all(f32[2,16,8,128]{3,2,0,1:T(8,128)S(1)} %copy.94), channel_id=1, replica_groups=mesh['gx'=16,'gy'=16] {'gx'}, dimensions={1} | all-to-all | bytes 262144 | tf_op jit(solution)/shard_map/all_to_all | solution.py:103
  39.8 0.0 copy-start.2
  39.8 1.0 %copy-done.2 = f32[16,128,128]{2,1,0:T(8,128)} copy-done((f32[16,128,128]{2,1,0:T(8,128)}, f32[16,128,128]{2,1,0:T(8,128)S(1)}, u32[]{:S(2)}) %copy-start.2) | copy-done | bytes 1048600
  40.7 0.6 %constant_dynamic-update-slice_fusion.38 = f32[16,128,128]{2,1,0:T(8,128)} fusion(f32[16,128,128]{2,1,0:T(8,128)} %copy-done.2, f32[2,16,8,128]{3,2,0,1:T(8,128)S(1)} %all_to_all.11), kind=kLoop, calls=%fused_computation.45 | loop fusion | bytes 131072 | tf_op jit(solution)/shard_map/stack | solution.py:108
  (35 shorter events, 0.6 us)
Async XLA Ops:
  0.9 7.4 %collective-permute-start = (f32[16,1,128]{2,1,0:T(1,128)S(1)}, f32[16,1,128]{2,1,0:T(1,128)S(1)}, u32[]{:S(2)}, u32[]{:S(2)}) collective-permute-start(f32[16,1,128]{2,1,0:T(1,128)S(1)} %get-tuple-element.128), channel_id=1, source_target_pairs={{0,1},{1,2},{2,3},{3,4},{4,5},{5,6},{6,7},{7,8},{8,9},{9,10},{10,1... | collective-permute-start | bytes 24584 | tf_op jit(solution)/shard_map/ppermute | solution.py:16
  2.8 5.5 %collective-permute-start.1 = (f32[16,1,128]{2,1,0:T(1,128)S(1)}, f32[16,1,128]{2,1,0:T(1,128)S(1)}, u32[]{:S(2)}, u32[]{:S(2)}) collective-permute-start(f32[16,1,128]{2,1,0:T(1,128)S(1)} %get-tuple-element.129), channel_id=1, source_target_pairs={{1,0},{2,1},{3,2},{4,3},{5,4},{6,5},{7,6},{8,7},{9,8},{10,9},{11,1... | collective-permute-start | bytes 24584 | tf_op jit(solution)/shard_map/ppermute | solution.py:17
  6.5 1.8 %copy-start = (f32[16,128,128]{2,1,0:T(8,128)S(1)}, f32[16,128,128]{2,1,0:T(8,128)}, u32[]{:S(2)}) copy-start(f32[16,128,128]{2,1,0:T(8,128)} %param.3) | copy-start | bytes 3145732
  6.5 1.9 %copy-start.1 = (f32[16,128,128]{2,1,0:T(8,128)S(1)}, f32[16,128,128]{2,1,0:T(8,128)}, u32[]{:S(2)}) copy-start(f32[16,128,128]{2,1,0:T(8,128)} %param.2) | copy-start | bytes 3145732
  39.8 1.0 %copy-start.2 = (f32[16,128,128]{2,1,0:T(8,128)}, f32[16,128,128]{2,1,0:T(8,128)S(1)}, u32[]{:S(2)}) copy-start(f32[16,128,128]{2,1,0:T(8,128)S(1)} %constant_dynamic-update-slice_fusion.39) | copy-start | bytes 3145732

commit v5 on v4

--- a/solution.py
+++ b/solution.py
@@ -78,24 +78,22 @@
     source_term = energy + y_weight * (padded[:, :-2] - 2.0 * energy + padded[:, 2:])
     s_loc, s_left, s_right = local_solve(coupling, source_term)
     n = height - 1
-    position = lax.axis_index("gx")
     own_face = coupling[height - 1]
-    lower_own = jnp.where(position == 0, 0.0, -own_face * s_left[n - 1])
+    coupled = -own_face * s_left[n - 1]
     middle_own = 1.0 + own_face - own_face * s_right[n - 1]
     target_own = source_term[height - 1] + own_face * s_loc[n - 1]
     face = coupling[0]
     middle_next = face - face * s_left[0]
-    upper_prev = -face * s_right[0]
     target_next = face * s_loc[0]
     parts = lax.axis_size("gx")
     chunk = width // parts
-    pack = jnp.stack([lower_own, middle_own, target_own, middle_next, upper_prev, target_next], 0)
-    pack = pack.reshape(6, parts, chunk, depth)
+    pack = jnp.stack([coupled, middle_own, target_own, middle_next, target_next], 0)
+    pack = pack.reshape(5, parts, chunk, depth)
     got = lax.all_to_all(pack, "gx", 1, 1, tiled=True)
-    lower = [got[0, p] for p in range(parts)]
+    lower = [None] + [got[0, p] for p in range(1, parts)]
     middle = [got[1, p] + got[3, p + 1] if p + 1 < parts else got[1, p] for p in range(parts)]
-    upper = [got[4, p + 1] for p in range(parts - 1)]
-    target = [got[2, p] + got[5, p + 1] if p + 1 < parts else got[2, p] for p in range(parts)]
+    upper = [got[0, p + 1] for p in range(parts - 1)]
+    target = [got[2, p] + got[4, p + 1] if p + 1 < parts else got[2, p] for p in range(parts)]
     solved = reduced_solve(lower, middle, upper, target)
     own = jnp.stack(solved, 0)
     prev = jnp.stack([solved[0] * 0.0] + solved[:-1], 0)

time: 41.6 us -> 40.6 us (0.976)
  blocking collectives: 29.4 us -> 28.4 us
    all_to_all x1, blocking collectives: 18.2 us -> 17.3 us  [body(): got = lax.all_to_all(pack, 'gx', 1, 1, tiled=True)]
    unnamed x22 -> x21, other arithmetic: 2.88 us -> 2.72 us
where the time goes in v5:
time: 40.6 us; the launch traced here: 40.3 us
  blocking collectives  28.4 us (70%)
  starting transfers between devices  5.69 us (14%)
  other arithmetic  3.39 us (8%)
  local copies, waits for them, and re-layouts  2.56 us (6%)
    all_to_all x1, blocking collectives, body(): got = lax.all_to_all(pack, 'gx', 1, 1, tiled=True)  17.3 us
    all_to_all x1, blocking collectives, body(): back = lax.all_to_all(back, 'gx', 1, 1, tiled=True)  11.1 us
    ppermute x1, starting transfers between devices, with_halo(): after = lax.ppermute(initial, axis, down)  3.77 us
    unnamed x21, other arithmetic  2.72 us
    ppermute x1, starting transfers between devices, with_halo(): before = lax.ppermute(last, axis, up)  1.92 us
    unnamed x21, local copies, waits for them, and re-layouts  1.03 us
    slice x1, local copies, waits for them, and re-layouts, with_halo(): last = lax.slice_in_dim(shard, length - width, length, axis=dim)  0.88 us
  transfers between devices with their start and end apart: 2, of which 0 were waited for; matrix products, arithmetic and copies ran while one was open for 4% of the time, Pallas kernels for 0%

profile of v5, /device:TPU:32, one launch (start us, length us, event | category | flops | bytes accessed | tf_op | source)
XLA Modules:
  0.0 40.3 jit_solution(12206443197563023483)
XLA Ops:
  0.0 0.9 %fusion.196 = (f32[16,1,128]{2,1,0:T(1,128)S(1)}, f32[16,1,128]{2,1,0:T(1,128)S(1)}) fusion(f32[16,128,128]{2,1,0:T(8,128)} %param.2), kind=kLoop, calls=%fused_computation.410 | loop fusion | bytes 32768 | tf_op jit(solution)/shard_map/slice | solution.py:14
  0.9 1.9 %collective-permute-start = (f32[16,1,128]{2,1,0:T(1,128)S(1)}, f32[16,1,128]{2,1,0:T(1,128)S(1)}, u32[]{:S(2)}, u32[]{:S(2)}) collective-permute-start(f32[16,1,128]{2,1,0:T(1,128)S(1)} %get-tuple-element.126), channel_id=1, source_target_pairs={{0,1},{1,2},{2,3},{3,4},{4,5},{5,6},{6,7},{7,8},{8,9},{9,10},{10,1... | collective-permute-start | bytes 24584 | tf_op jit(solution)/shard_map/ppermute | solution.py:16
  2.8 0.0 copy-start
  2.8 0.0 copy-start.1
  2.8 3.8 %collective-permute-start.1 = (f32[16,1,128]{2,1,0:T(1,128)S(1)}, f32[16,1,128]{2,1,0:T(1,128)S(1)}, u32[]{:S(2)}, u32[]{:S(2)}) collective-permute-start(f32[16,1,128]{2,1,0:T(1,128)S(1)} %get-tuple-element.127), channel_id=1, source_target_pairs={{1,0},{2,1},{3,2},{4,3},{5,4},{6,5},{7,6},{8,7},{9,8},{10,9},{11,1... | collective-permute-start | bytes 24584 | tf_op jit(solution)/shard_map/ppermute | solution.py:17
  6.6 1.6 %constant_dynamic-update-slice_fusion.4 = (f32[5,16,8,128]{3,2,0,1:T(8,128)S(1)}, f32[1,128,128]{2,1,0:T(8,128)S(1)}, f32[1,128,128]{2,1,0:T(8,128)S(1)}, f32[1,...) fusion(f32[16,128,128]{2,1,0:T(8,128)} %param.3), kind=kLoop, calls=%fused_computation.11 | loop fusion | flops 2162687 | bytes 3538944
  8.3 0.0 copy-done
  8.3 0.0 collective-permute-done
  8.3 0.0 collective-permute-done.1
  8.3 0.0 copy-done.1
  8.3 0.3 fusion.2
  8.7 0.2 constant_dynamic-update-slice_fusion.2
  8.9 0.2 constant_dynamic-update-slice_fusion.1
  9.1 0.2 constant_dynamic-update-slice_fusion
  9.2 17.3 %all_to_all.10 = f32[5,16,8,128]{3,2,0,1:T(8,128)S(1)} all-to-all(f32[5,16,8,128]{3,2,0,1:T(8,128)S(1)} %get-tuple-element.55), channel_id=1, replica_groups=mesh['gx'=16,'gy'=16] {'gx'}, dimensions={1} | all-to-all | bytes 655360 | tf_op jit(solution)/shard_map/all_to_all | solution.py:92
  26.5 0.1 fusion.35
  26.6 0.1 fusion.47
  26.7 0.1 constant_dynamic-update-slice_fusion.20
  27.0 11.1 %all_to_all.11 = f32[2,16,8,128]{3,2,0,1:T(8,128)S(1)} all-to-all(f32[2,16,8,128]{3,2,0,1:T(8,128)S(1)} %copy.79), channel_id=1, replica_groups=mesh['gx'=16,'gy'=16] {'gx'}, dimensions={1} | all-to-all | bytes 262144 | tf_op jit(solution)/shard_map/all_to_all | solution.py:101
  38.1 0.1 constant_dynamic-update-slice_fusion.52
  38.7 0.0 copy-start.2
  38.7 1.0 %copy-done.2 = f32[16,128,128]{2,1,0:T(8,128)} copy-done((f32[16,128,128]{2,1,0:T(8,128)}, f32[16,128,128]{2,1,0:T(8,128)S(1)}, u32[]{:S(2)}) %copy-start.2) | copy-done | bytes 1048600
  39.7 0.6 %constant_dynamic-update-slice_fusion.37 = f32[16,128,128]{2,1,0:T(8,128)} fusion(f32[16,128,128]{2,1,0:T(8,128)} %copy-done.2, f32[2,16,8,128]{3,2,0,1:T(8,128)S(1)} %all_to_all.11), kind=kLoop, calls=%fused_computation.44 | loop fusion | bytes 131072 | tf_op jit(solution)/shard_map/stack | solution.py:106
  (34 shorter events, 0.6 us)
Async XLA Ops:
  0.9 7.4 %collective-permute-start = (f32[16,1,128]{2,1,0:T(1,128)S(1)}, f32[16,1,128]{2,1,0:T(1,128)S(1)}, u32[]{:S(2)}, u32[]{:S(2)}) collective-permute-start(f32[16,1,128]{2,1,0:T(1,128)S(1)} %get-tuple-element.126), channel_id=1, source_target_pairs={{0,1},{1,2},{2,3},{3,4},{4,5},{5,6},{6,7},{7,8},{8,9},{9,10},{10,1... | collective-permute-start | bytes 24584 | tf_op jit(solution)/shard_map/ppermute | solution.py:16
  2.8 5.5 %copy-start = (f32[16,128,128]{2,1,0:T(8,128)S(1)}, f32[16,128,128]{2,1,0:T(8,128)}, u32[]{:S(2)}) copy-start(f32[16,128,128]{2,1,0:T(8,128)} %param.3) | copy-start | bytes 3145732
  2.8 5.5 %copy-start.1 = (f32[16,128,128]{2,1,0:T(8,128)S(1)}, f32[16,128,128]{2,1,0:T(8,128)}, u32[]{:S(2)}) copy-start(f32[16,128,128]{2,1,0:T(8,128)} %param.2) | copy-start | bytes 3145732
  2.8 5.5 %collective-permute-start.1 = (f32[16,1,128]{2,1,0:T(1,128)S(1)}, f32[16,1,128]{2,1,0:T(1,128)S(1)}, u32[]{:S(2)}, u32[]{:S(2)}) collective-permute-start(f32[16,1,128]{2,1,0:T(1,128)S(1)} %get-tuple-element.127), channel_id=1, source_target_pairs={{1,0},{2,1},{3,2},{4,3},{5,4},{6,5},{7,6},{8,7},{9,8},{10,9},{11,1... | collective-permute-start | bytes 24584 | tf_op jit(solution)/shard_map/ppermute | solution.py:17
  38.7 1.0 %copy-start.2 = (f32[16,128,128]{2,1,0:T(8,128)}, f32[16,128,128]{2,1,0:T(8,128)S(1)}, u32[]{:S(2)}) copy-start(f32[16,128,128]{2,1,0:T(8,128)S(1)} %constant_dynamic-update-slice_fusion.38) | copy-start | bytes 3145732

commit v6 on v5

--- a/solution.py
+++ b/solution.py
@@ -74,7 +74,12 @@
 
 def body(energy, coupling):
     height, width, depth = energy.shape
-    padded = with_halo(energy, (("gy", 1),), 1)
+    size = lax.axis_size("gy")
+    up = [(i, i + 1) for i in range(size - 1)]
+    down = [(i + 1, i) for i in range(size - 1)]
+    before = lax.ppermute(energy[:, width - 1], "gy", up)
+    after = lax.ppermute(energy[:, 0], "gy", down)
+    padded = jnp.concatenate([before[:, None], energy, after[:, None]], 1)
     source_term = energy + y_weight * (padded[:, :-2] - 2.0 * energy + padded[:, 2:])
     s_loc, s_left, s_right = local_solve(coupling, source_term)
     n = height - 1

time: 40.6 us -> 39.9 us (0.983)
  starting transfers between devices: 5.69 us -> 4.46 us
  waiting for transfers between devices: 0.01 us -> 1.04 us
  blocking collectives: 28.4 us -> 27.8 us
    ppermute x2, starting transfers between devices: 5.69 us -> 4.46 us  [the longest x1 2.54 us: body(): before = lax.ppermute(energy[:, width - 1], 'gy', up)]
    ppermute x2, waiting for transfers between devices: 0.01 us -> 1.04 us  [the longest x1 1.04 us: body(): before = lax.ppermute(energy[:, width - 1], 'gy', up)]
  transfers between devices with their start and end apart: 2 -> 2, of which waited for: 0 -> 1; matrix products, arithmetic and copies ran while one was open for 4% -> 4% of each run, Pallas kernels for 0% -> 0%
where the time goes in v6:
time: 39.9 us; the launch traced here: 39.5 us
  blocking collectives  27.8 us (70%)
  starting transfers between devices  4.46 us (11%)
  other arithmetic  3.39 us (8%)
  local copies, waits for them, and re-layouts  2.56 us (6%)
  waiting for transfers between devices  1.04 us (3%)
    all_to_all x1, blocking collectives, body(): got = lax.all_to_all(pack, 'gx', 1, 1, tiled=True)  16.9 us
    all_to_all x1, blocking collectives, body(): back = lax.all_to_all(back, 'gx', 1, 1, tiled=True)  10.9 us
    unnamed x21, other arithmetic  2.72 us
    ppermute x1, starting transfers between devices, body(): before = lax.ppermute(energy[:, width - 1], 'gy', up)  2.54 us
    ppermute x1, starting transfers between devices, body(): after = lax.ppermute(energy[:, 0], 'gy', down)  1.92 us
    ppermute x1, waiting for transfers between devices, body(): before = lax.ppermute(energy[:, width - 1], 'gy', up)  1.04 us
    unnamed x21, local copies, waits for them, and re-layouts  1.03 us
    slice x1, local copies, waits for them, and re-layouts, body(): before = lax.ppermute(energy[:, width - 1], 'gy', up)  0.88 us
  transfers between devices with their start and end apart: 2, of which 1 were waited for; matrix products, arithmetic and copies ran while one was open for 4% of the time, Pallas kernels for 0%

profile of v6, /device:TPU:32, one launch (start us, length us, event | category | flops | bytes accessed | tf_op | source)
XLA Modules:
  0.0 39.5 jit_solution(216629959845590475)
XLA Ops:
  0.0 0.9 %fusion.196 = (f32[16,1,128]{2,1,0:T(1,128)S(1)}, f32[16,1,128]{2,1,0:T(1,128)S(1)}) fusion(f32[16,128,128]{2,1,0:T(8,128)} %param.2), kind=kLoop, calls=%fused_computation.410 | loop fusion | bytes 32768 | tf_op jit(solution)/shard_map/slice | solution.py:80
  0.9 1.9 %collective-permute-start.1 = (f32[16,128]{1,0:T(8,128)S(1)}, f32[16,128]{1,0:T(8,128)S(1)}, u32[]{:S(2)}, u32[]{:S(2)}) collective-permute-start(f32[16,128]{1,0:T(8,128)S(1)} %bitcast.1103), channel_id=1, source_target_pairs={{1,0},{2,1},{3,2},{4,3},{5,4},{6,5},{7,6},{8,7},{9,8},{10,9},{11,1... | collective-permute-start | bytes 24584 | tf_op jit(solution)/shard_map/ppermute | solution.py:81
  2.8 0.0 copy-start
  2.8 0.0 copy-start.1
  2.8 2.5 %collective-permute-start = (f32[16,128]{1,0:T(8,128)S(1)}, f32[16,128]{1,0:T(8,128)S(1)}, u32[]{:S(2)}, u32[]{:S(2)}) collective-permute-start(f32[16,128]{1,0:T(8,128)S(1)} %bitcast.1102), channel_id=1, source_target_pairs={{0,1},{1,2},{2,3},{3,4},{4,5},{5,6},{6,7},{7,8},{8,9},{9,10},{10,1... | collective-permute-start | bytes 24584 | tf_op jit(solution)/shard_map/ppermute | solution.py:80
  5.4 1.6 %constant_dynamic-update-slice_fusion.4 = (f32[5,16,8,128]{3,2,0,1:T(8,128)S(1)}, f32[1,128,128]{2,1,0:T(8,128)S(1)}, f32[1,128,128]{2,1,0:T(8,128)S(1)}, f32[1,...) fusion(f32[16,128,128]{2,1,0:T(8,128)} %param.3), kind=kLoop, calls=%fused_computation.11 | loop fusion | flops 2162687 | bytes 3538944
  7.0 0.0 copy-done
  7.1 0.0 collective-permute-done.1
  7.1 1.0 %collective-permute-done = f32[16,128]{1,0:T(8,128)S(1)} collective-permute-done((f32[16,128]{1,0:T(8,128)S(1)}, f32[16,128]{1,0:T(8,128)S(1)}, u32[]{:S(2)}, u32[]{:S(2)}) %collective-permute-start) | collective-permute-done | bytes 8224 | tf_op jit(solution)/shard_map/ppermute | solution.py:80
  8.1 0.0 copy-done.1
  8.1 0.3 fusion.2
  8.5 0.2 constant_dynamic-update-slice_fusion.2
  8.7 0.2 constant_dynamic-update-slice_fusion.1
  8.8 0.2 constant_dynamic-update-slice_fusion
  9.0 16.9 %all_to_all.10 = f32[5,16,8,128]{3,2,0,1:T(8,128)S(1)} all-to-all(f32[5,16,8,128]{3,2,0,1:T(8,128)S(1)} %get-tuple-element.55), channel_id=1, replica_groups=mesh['gx'=16,'gy'=16] {'gx'}, dimensions={1} | all-to-all | bytes 655360 | tf_op jit(solution)/shard_map/all_to_all | solution.py:97
  25.9 0.1 fusion.35
  26.0 0.1 fusion.47
  26.1 0.1 constant_dynamic-update-slice_fusion.20
  26.4 10.9 %all_to_all.11 = f32[2,16,8,128]{3,2,0,1:T(8,128)S(1)} all-to-all(f32[2,16,8,128]{3,2,0,1:T(8,128)S(1)} %copy.83), channel_id=1, replica_groups=mesh['gx'=16,'gy'=16] {'gx'}, dimensions={1} | all-to-all | bytes 262144 | tf_op jit(solution)/shard_map/all_to_all | solution.py:106
  37.3 0.1 constant_dynamic-update-slice_fusion.52
  37.9 0.0 copy-start.2
  37.9 1.0 %copy-done.2 = f32[16,128,128]{2,1,0:T(8,128)} copy-done((f32[16,128,128]{2,1,0:T(8,128)}, f32[16,128,128]{2,1,0:T(8,128)S(1)}, u32[]{:S(2)}) %copy-start.2) | copy-done | bytes 1048600
  38.8 0.6 %constant_dynamic-update-slice_fusion.37 = f32[16,128,128]{2,1,0:T(8,128)} fusion(f32[16,128,128]{2,1,0:T(8,128)} %copy-done.2, f32[2,16,8,128]{3,2,0,1:T(8,128)S(1)} %all_to_all.11), kind=kLoop, calls=%fused_computation.44 | loop fusion | bytes 131072 | tf_op jit(solution)/shard_map/stack | solution.py:111
  (34 shorter events, 0.6 us)
Async XLA Ops:
  0.9 6.2 %collective-permute-start.1 = (f32[16,128]{1,0:T(8,128)S(1)}, f32[16,128]{1,0:T(8,128)S(1)}, u32[]{:S(2)}, u32[]{:S(2)}) collective-permute-start(f32[16,128]{1,0:T(8,128)S(1)} %bitcast.1103), channel_id=1, source_target_pairs={{1,0},{2,1},{3,2},{4,3},{5,4},{6,5},{7,6},{8,7},{9,8},{10,9},{11,1... | collective-permute-start | bytes 24584 | tf_op jit(solution)/shard_map/ppermute | solution.py:81
  2.8 4.2 %copy-start = (f32[16,128,128]{2,1,0:T(8,128)S(1)}, f32[16,128,128]{2,1,0:T(8,128)}, u32[]{:S(2)}) copy-start(f32[16,128,128]{2,1,0:T(8,128)} %param.3) | copy-start | bytes 3145732
  2.8 5.3 %copy-start.1 = (f32[16,128,128]{2,1,0:T(8,128)S(1)}, f32[16,128,128]{2,1,0:T(8,128)}, u32[]{:S(2)}) copy-start(f32[16,128,128]{2,1,0:T(8,128)} %param.2) | copy-start | bytes 3145732
  2.8 5.3 %collective-permute-start = (f32[16,128]{1,0:T(8,128)S(1)}, f32[16,128]{1,0:T(8,128)S(1)}, u32[]{:S(2)}, u32[]{:S(2)}) collective-permute-start(f32[16,128]{1,0:T(8,128)S(1)} %bitcast.1102), channel_id=1, source_target_pairs={{0,1},{1,2},{2,3},{3,4},{4,5},{5,6},{6,7},{7,8},{8,9},{9,10},{10,1... | collective-permute-start | bytes 24584 | tf_op jit(solution)/shard_map/ppermute | solution.py:80
  37.9 1.0 %copy-start.2 = (f32[16,128,128]{2,1,0:T(8,128)}, f32[16,128,128]{2,1,0:T(8,128)S(1)}, u32[]{:S(2)}) copy-start(f32[16,128,128]{2,1,0:T(8,128)S(1)} %constant_dynamic-update-slice_fusion.38) | copy-start | bytes 3145732
